TPU v7x, 128 devices: a whole 4x4x4 slice. The times are simulated.
128 devices in a mesh: pool: 4 (over x_hi, core), grp: 4 (over y), tp: 8 (over z, x_lo).
Axes of the slice: x: 4 (x_hi: 2, x_lo: 2; x = x_hi * 2 + x_lo), y: 4, z: 4, core: 2. Of those that a mesh axis runs over, the one named last changes fastest.
Arguments:
- hidden: bfloat16 [1024, 8192], P('pool', 'grp'), may hold values from -6 to 6
- attn_gain: float32 [8192], P('grp'), may hold values from 0.25 to 1.75
- w_query: bfloat16 [8192, 8192], P('grp', 'tp'), may hold values from -0.0625 to 0.0625
- w_key: bfloat16 [8192, 1024], P('grp', 'tp'), may hold values from -1 to 1
- w_value: bfloat16 [8192, 1024], P('grp', 'tp'), may hold values from -0.0625 to 0.0625
- w_out: bfloat16 [8192, 8192], P('tp', 'grp'), may hold values from -0.0625 to 0.0625
- prefix_keys: bfloat16 [8, 16384, 1024], P('pool', 'grp', 'tp'), may hold values from -300 to 300
- prefix_values: bfloat16 [8, 16384, 1024], P('pool', 'grp', 'tp'), may hold values from -6 to 6
- suffix_keys: bfloat16 [1024, 256, 1024], P('pool', 'grp', 'tp'), may hold values from -300 to 300
- suffix_values: bfloat16 [1024, 256, 1024], P('pool', 'grp', 'tp'), may hold values from -6 to 6
- prefix_ids: int32 [1024], P('pool'), may hold values from 0 to 7, as said below
- suffix_lens: int32 [1024], P('pool'), may hold values from 1 to 256, as said below
- ffn_gain: float32 [8192], P('grp'), may hold values from 0.25 to 1.75
- w_gate: bfloat16 [8192, 14336], P('grp', ('pool', 'tp')), may hold values from -0.0625 to 0.0625
- w_up: bfloat16 [8192, 14336], P('grp', ('pool', 'tp')), may hold values from -0.0625 to 0.0625
- w_down: bfloat16 [14336, 8192], P(('pool', 'tp'), 'grp'), may hold values from -0.046875 to 0.046875
Outputs:
- result: bfloat16 [1024, 8192], P(('pool', 'tp'), 'grp')
Inputs may be any that keep to these rules, and one draw needn't show every extreme that they name: `prefix_ids`: within rows p * 256 to (p + 1) * 256 - 1, each of the prefixes p * 2 to (p + 1) * 2 - 1 is named by exactly 128 streams, and no other prefix is named. `suffix_lens`: each block of 256 streams holds a stream of length 256 and one of length 1.
All inputs are finite; a program needn't handle non-finite values.
Results may differ from a plain program's by a relative error of at most 0.015.
Values may be sent and summed in bfloat16 or wider, within the bound.
No kernel may reach another device: no remote copies, remote signals or barrier semaphores. Data moves between devices by JAX's collectives and lax.ppermute only.
A program may use at most 192 MiB of HBM per device.

v0:
```python
import math
import jax
import jax.numpy as jnp
from jax import lax
from jax.sharding import PartitionSpec as P

D = 8192
HD = 128
epsilon = 1e-05


def joined(array, axis, combine):
    everything = jax.tree.map(lambda part: lax.all_gather(part, axis), array)
    first = jax.tree.map(lambda part: part[0], everything)

    def lap(k, so_far):
        return combine(so_far, jax.tree.map(lambda part: part[k], everything))

    return lax.fori_loop(1, lax.axis_size(axis), lap, first)


def combine_parts(earlier, later):
    peak_one, total_one, numer_one = earlier
    peak_two, total_two, numer_two = later
    peak = jnp.maximum(peak_one, peak_two)
    scale_one = jnp.exp(peak_one - peak)
    scale_two = jnp.exp(peak_two - peak)
    total = total_one * scale_one + total_two * scale_two
    numer = numer_one * scale_one[..., None] + numer_two * scale_two[..., None]
    return (peak, total, numer)


def body(
    hidden,
    attn_gain,
    w_query,
    w_key,
    w_value,
    w_out,
    prefix_keys,
    prefix_values,
    suffix_keys,
    suffix_values,
    prefix_ids,
    suffix_lens,
    ffn_gain,
    w_gate,
    w_up,
    w_down,
):
    stream_count = hidden.shape[0]
    hidden_float = hidden.astype(jnp.float32)
    squares = lax.psum(jnp.sum(hidden_float * hidden_float, axis=1), "grp")
    inverse = lax.rsqrt(squares / D + epsilon)
    normed = (hidden_float * inverse[:, None] * attn_gain).astype(jnp.bfloat16)
    part_query = jnp.dot(normed, w_query, preferred_element_type=jnp.float32)
    part_key = jnp.dot(normed, w_key, preferred_element_type=jnp.float32)
    part_value = jnp.dot(normed, w_value, preferred_element_type=jnp.float32)
    query, key_new, value_new = lax.psum((part_query, part_key, part_value), "grp")
    query = query.astype(jnp.bfloat16)
    key_new = key_new.astype(jnp.bfloat16)
    value_new = value_new.astype(jnp.bfloat16)
    kv_local = w_key.shape[1] // HD
    q_local = w_query.shape[1] // HD
    groups = q_local // kv_local
    prefix_local = prefix_keys.shape[0]
    pre_length = prefix_keys.shape[1]
    suf_length = suffix_keys.shape[1]
    factor = 1.0 / math.sqrt(HD)
    heads = query.reshape(stream_count, kv_local, groups, HD)
    pre_key = prefix_keys.reshape(prefix_local, pre_length, kv_local, HD)
    pre_value = prefix_values.reshape(prefix_local, pre_length, kv_local, HD)
    suf_key = suffix_keys.reshape(stream_count, suf_length, kv_local, HD)
    suf_value = suffix_values.reshape(stream_count, suf_length, kv_local, HD)
    local_prefix = prefix_ids - lax.axis_index("pool") * prefix_local
    per_group = stream_count // prefix_local
    one_hot = (local_prefix[:, None] == jnp.arange(prefix_local, dtype=jnp.int32)[None, :]).astype(
        jnp.int32
    )
    rank_within = jnp.sum(jnp.cumsum(one_hot, axis=0) * one_hot, axis=1) - 1
    target = local_prefix * per_group + rank_within
    group_order = (
        jnp.zeros((stream_count,), jnp.int32)
        .at[target]
        .set(jnp.arange(stream_count, dtype=jnp.int32))
    )
    grouped = heads[group_order].reshape(prefix_local, per_group, kv_local, groups, HD)
    pre_scores = (
        jnp.einsum("pskgd,pjkd->pskgj", grouped, pre_key, preferred_element_type=jnp.float32)
        * factor
    )
    pre_peak = pre_scores.max(axis=4).reshape(stream_count, kv_local, groups)[target]
    positions = lax.axis_index("grp") * suf_length + jnp.arange(suf_length, dtype=jnp.int32)
    valid = (positions[None, :] < suffix_lens[:, None])[:, None, None, :]
    suf_scores = (
        jnp.einsum("skgd,sjkd->skgj", heads, suf_key, preferred_element_type=jnp.float32) * factor
    )
    suf_scores = jnp.where(valid, suf_scores, -1e30)
    peak = jnp.maximum(pre_peak, suf_scores.max(axis=3))
    peak_grouped = peak[group_order].reshape(prefix_local, per_group, kv_local, groups)
    pre_weights = jnp.exp(pre_scores - peak_grouped[..., None]).astype(jnp.bfloat16)
    pre_total = (
        pre_weights.astype(jnp.float32).sum(axis=4).reshape(stream_count, kv_local, groups)[target]
    )
    pre_numer = jnp.einsum(
        "pskgj,pjkd->pskgd", pre_weights, pre_value, preferred_element_type=jnp.float32
    )
    pre_numer = pre_numer.reshape(stream_count, kv_local, groups, HD)[target]
    suf_weights = jnp.where(valid, jnp.exp(suf_scores - peak[:, :, :, None]), 0.0).astype(
        jnp.bfloat16
    )
    total = pre_total + suf_weights.astype(jnp.float32).sum(axis=3)
    numer = pre_numer + jnp.einsum(
        "skgj,sjkd->skgd", suf_weights, suf_value, preferred_element_type=jnp.float32
    )
    peak, total, numer = joined((peak, total, numer), "grp", combine_parts)
    own_score = (
        jnp.einsum(
            "skgd,skd->skg",
            heads,
            key_new.reshape(stream_count, kv_local, HD),
            preferred_element_type=jnp.float32,
        )
        * factor
    )
    new_peak = jnp.maximum(peak, own_score)
    rescale = jnp.exp(peak - new_peak)
    own_weight = jnp.exp(own_score - new_peak).astype(jnp.bfloat16).astype(jnp.float32)
    total = total * rescale + own_weight
    own_value = value_new.reshape(stream_count, kv_local, 1, HD).astype(jnp.float32)
    numer = numer * rescale[..., None] + own_weight[..., None] * own_value
    attended = (numer / total[..., None]).reshape(stream_count, q_local * HD).astype(jnp.bfloat16)
    partial_out = jnp.dot(attended, w_out, preferred_element_type=jnp.float32)
    share = stream_count // lax.axis_size("tp")
    tp_start = lax.axis_index("tp") * share
    summed = lax.psum(partial_out, "tp")
    summed = lax.dynamic_slice_in_dim(summed, tp_start, share, 0)
    own_hidden = lax.dynamic_slice_in_dim(hidden_float, tp_start, share, 0)
    middle = (own_hidden + summed).astype(jnp.bfloat16)
    gathered = lax.all_gather(middle, ("pool", "tp"), axis=0, tiled=True)
    gathered_float = gathered.astype(jnp.float32)
    ffn_squares = lax.psum(jnp.sum(gathered_float * gathered_float, axis=1), "grp")
    ffn_inverse = lax.rsqrt(ffn_squares / D + epsilon)
    normed_ffn = (gathered_float * ffn_inverse[:, None] * ffn_gain).astype(jnp.bfloat16)
    part_gate = jnp.dot(normed_ffn, w_gate, preferred_element_type=jnp.float32)
    part_upward = jnp.dot(normed_ffn, w_up, preferred_element_type=jnp.float32)
    gate, upward = lax.psum((part_gate, part_upward), "grp")
    act = (jax.nn.silu(gate) * upward).astype(jnp.bfloat16)
    returned = lax.psum_scatter(
        jnp.dot(act, w_down, preferred_element_type=jnp.float32),
        ("pool", "tp"),
        scatter_dimension=0,
        tiled=True,
    )
    return (middle.astype(jnp.float32) + returned).astype(jnp.bfloat16)


def solution(mesh):
    return jax.shard_map(
        body,
        mesh=mesh,
        in_specs=(
            P("pool", "grp"),
            P("grp"),
            P("grp", "tp"),
            P("grp", "tp"),
            P("grp", "tp"),
            P("tp", "grp"),
            P("pool", "grp", "tp"),
            P("pool", "grp", "tp"),
            P("pool", "grp", "tp"),
            P("pool", "grp", "tp"),
            P("pool"),
            P("pool"),
            P("grp"),
            P("grp", ("pool", "tp")),
            P("grp", ("pool", "tp")),
            P(("pool", "tp"), "grp"),
        ),
        out_specs=P(("pool", "tp"), "grp"),
        check_vma=False,
    )
```

profile of v0, /device:TPU:1, one launch (start us, length us, event | category | flops | bytes accessed | tf_op | source)
XLA Modules:
  0.0 672.8 jit_solution(15598244335575411505)
XLA Ops:
  6.5 0.8 fusion.59
  7.4 0.7 broadcast_subtract_fusion
  8.1 1.6 multiply_reduce_fusion
  9.7 9.5 %psum.56 = f32[256]{0:T(256)S(1)} all-reduce(f32[256]{0:T(256)S(1)} %multiply_reduce_fusion), channel_id=1, replica_groups=mesh['pool'=4,'grp'=4,'tp'=8] {'grp'}, use_global_device_ids=true, to_apply=%region_1.0 | all-reduce | flops 256 | bytes 2048 | tf_op jit(solution)/shard_map/psum | solution.py:53
  19.2 4.9 fusion.46
  24.1 0.5 fusion.45
  24.7 0.5 fusion.44
  25.2 26.5 %all-reduce.9 = (bf16[256,1024]{1,0:T(8,128)(2,1)S(1)}, bf16[256,128]{1,0:T(8,128)(2,1)S(1)}, bf16[256,128]{1,0:T(8,128)(2,1)S(1)}) all-reduce(f32[256,1024]{1,0:T(8,128)} %fusion.46, f32[256,128]{1,0:T(8,128)S(1)} %fusion.45, f32[256,128]{1,0:T(8,128)S(1)} %fusion.44), channel_id=1, replica_groups=mesh['pool'=4,'grp'=4,'tp'=8] {'grp'}, use_global_device_ids=true, to_apply=%region_2.0 | all-reduce | flops 327680 | bytes 1966080 | tf_op jit(solution)/shard_map/psum | solution.py:59
  51.7 0.1 copy.64
  51.8 0.6 reduce-window.6
  52.4 0.2 slice_reduce_fusion
  52.6 0.2 reduce-window.9
  52.8 0.1 add_bitcast_fusion
  53.0 1.6 scatter_custom_fusion
  54.6 0.8 gather_fusion
  55.4 13.1 %bitcast_reduce_fusion = (f32[2,128,8]{1,2,0:T(8,128)S(1)}, f32[2,128,8,4096]{3,1,2,0:T(8,128)}) fusion(bf16[2,4096,128]{2,1,0:T(8,128)(2,1)S(1)} %copy-done, bf16[2,128,8,128]{3,2,1,0:T(8,128)(2,1)S(1)} %bitcast.165), kind=kOutput, calls=%fused_computation.17 | convolution fusion | flops 2164258816 | bytes 36184064 | tf_op jit(solution)/shard_map/pskgd,pjkd->pskgj/dot_general | solution.py:89
  68.5 0.1 copy.47
  68.6 0.7 gather_fusion.1
  69.4 0.1 broadcast_compare_fusion
  69.5 4.5 fusion.47
  74.1 0.7 gather_fusion.2
  74.9 13.8 %fusion.17 = f32[2,128,1,8,128]{4,1,3,0,2:T(8,128)S(1)} fusion(bf16[2,4096,128]{2,1,0:T(8,128)(2,1)} %param.25, f32[2,128,8]{1,2,0:T(8,128)S(1)} %copy.48, f32[2,128,8,4096]{3,1,2,0:T(8,128)} %get-tuple-element.234), kind=kOutput, calls=%fused_computation.37 | convolution fusion | flops 2172649472 | bytes 36708352 | tf_op jit(solution)/shard_map/pskgj,pjkd->pskgd/dot_general | solution.py:105
  88.7 1.6 copy.50
  90.3 2.9 gather_fusion.4
  93.2 4.7 convolution_add_fusion
  98.0 10.4 %all-gather.1 = f32[1024,8]{1,0:T(8,128)S(1)} all-gather(f32[256,8]{1,0:T(8,128)S(1)} %max.43), channel_id=3, replica_groups=mesh['pool'=4,'grp'=4,'tp'=8] {'grp'}, dimensions={0}, use_global_device_ids=true | all-gather | bytes 40960 | tf_op jit(solution)/shard_map/all_gather | solution.py:13
  108.5 14.6 %convert_reduce_fusion = f32[2,128,8]{1,2,0:T(8,128)S(1)} fusion(f32[2,128,8]{1,2,0:T(8,128)S(1)} %copy.48, f32[2,128,8,4096]{3,1,2,0:T(8,128)} %get-tuple-element.234), kind=kLoop, calls=%fused_computation.20 | loop fusion | flops 41940992 | bytes 33570816 | tf_op jit(solution)/shard_map/reduce_sum | solution.py:103
  123.2 0.1 copy.49
  123.3 0.7 gather_fusion.3
  124.0 0.7 convert_reduce_fusion.1
  124.8 14.8 %all-gather.2 = f32[1024,8]{1,0:T(8,128)S(1)} all-gather(f32[256,8]{1,0:T(8,128)S(1)} %add.162), channel_id=4, replica_groups=mesh['pool'=4,'grp'=4,'tp'=8] {'grp'}, dimensions={0}, use_global_device_ids=true | all-gather | bytes 40960 | tf_op jit(solution)/shard_map/all_gather | solution.py:13
  139.7 0.2 copy.54
  139.8 0.2 copy.55
  140.0 0.4 fusion.32
  140.4 0.1 copy.63
  140.5 16.9 %all-gather.8.cloned.1.call-done = f32[1024,8,128]{2,1,0:T(8,128)} async-done(((f32[256,8,128]{2,1,0:T(8,128)}), f32[1024,8,128]{2,1,0:T(8,128)}) %all-gather.8.cloned.1.call-update) | async-done | bytes 4194320 | tf_op jit(solution)/shard_map/all_gather | solution.py:13
  157.4 1.3 slice_bitcast_fusion
  158.7 6.7 while.19
  158.8 0.1 copy.80
  158.9 0.1 copy.81
  159.0 1.9 fusion.65
  161.0 0.1 copy.80
  161.1 0.1 copy.81
  161.3 1.9 fusion.65
  163.3 0.1 copy.80
  163.4 0.1 copy.81
  163.5 1.9 fusion.65
  165.4 0.1 copy.59
  165.6 0.1 copy.58
  165.7 0.1 copy.57
  165.8 1.0 divide_convert_fusion
  166.9 4.8 fusion.28
  171.8 1.6 convert_element_type.68
  173.4 103.1 %all-reduce.6.cloned.1.call-done = f32[256,2048]{1,0:T(8,128)} async-done(((f32[256,2048]{1,0:T(8,128)}), f32[256,2048]{1,0:T(8,128)}) %all-reduce.6.cloned.1.call-update) | async-done | bytes 2097168 | tf_op jit(solution)/shard_map/psum | solution.py:136
  276.5 1.7 add_convert_fusion.1
  278.2 85.9 %all-gather.6.cloned.1.call-done = bf16[1024,2048]{1,0:T(8,128)(2,1)} async-done(((bf16[32,2048]{1,0:T(8,128)(2,1)}), bf16[1024,2048]{1,0:T(8,128)(2,1)}) %all-gather.6.cloned.1.call-update) | async-done | bytes 4194320 | tf_op jit(solution)/shard_map/all_gather | solution.py:140
  364.2 3.1 fusion.9
  367.2 8.5 %psum.61 = f32[1024]{0:T(1024)S(1)} all-reduce(f32[1024]{0:T(1024)S(1)} %fusion.9), channel_id=1, replica_groups=mesh['pool'=4,'grp'=4,'tp'=8] {'grp'}, use_global_device_ids=true, to_apply=%region_17.18 | all-reduce | flops 1024 | bytes 8192 | tf_op jit(solution)/shard_map/psum | solution.py:142
  375.7 6.4 fusion.22
  382.1 3.5 fusion.24
  385.6 85.0 %all-reduce.8.cloned.1.call-done = (f32[1024,448]{0,1:T(8,128)}, f32[1024,448]{0,1:T(8,128)}) async-done(((f32[1024,448]{0,1:T(8,128)}, f32[1024,448]{0,1:T(8,128)}), (f32[1024,448]{0,1:T(8,128)}, f32[1024,448]{0,1:T(8,128)})) %all-reduce.8.cloned.1.call-update) | async-done | bytes 3670032 | tf_op jit(solution)/shard_map/psum | solution.py:147
  470.7 8.3 %fusion.26 = f32[1024,2048]{1,0:T(8,128)} fusion(bf16[448,2048]{1,0:T(8,128)(2,1)} %param.33, f32[1024,448]{0,1:T(8,128)} %get-tuple-element.224, f32[1024,448]{0,1:T(8,128)} %get-tuple-element.225), kind=kOutput, calls=%fused_computation.44 | convolution fusion | flops 1881800704 | bytes 13893632 | tf_op jit(solution)/shard_map/dot_general | solution.py:150
  478.9 185.7 %reduce-scatter.2.cloned.1.call-done = f32[32,2048]{1,0:T(8,128)} async-done(((f32[1024,2048]{1,0:T(8,128)}), f32[32,2048]{1,0:T(8,128)}) %reduce-scatter.2.cloned.1.call-update) | async-done | bytes 262160 | tf_op jit(solution)/shard_map/reduce_scatter | solution.py:149
  664.6 1.6 add_convert_fusion
  (64 shorter events, 0.8 us)
Async XLA Ops:
  6.5 48.9 %copy-start = (bf16[2,4096,128]{2,1,0:T(8,128)(2,1)S(1)}, bf16[2,4096,128]{2,1,0:T(8,128)(2,1)}, u32[]{:S(2)}) copy-start(bf16[2,4096,128]{2,1,0:T(8,128)(2,1)} %param.24) | copy-start | bytes 6291460
  6.5 150.9 %all-gather.8.cloned.1.call-start = ((), (), s32[]{:S(2)}) async-start(), calls=%async_computation.4 | async-start | bytes 5242880 | tf_op jit(solution)/shard_map/all_gather | solution.py:13
  8.1 16.1 %copy-start.2 = (bf16[256,2048]{1,0:T(8,128)(2,1)S(1)}, bf16[256,2048]{1,0:T(8,128)(2,1)}, u32[]{:S(2)}) copy-start(bf16[256,2048]{1,0:T(8,128)(2,1)} %param.18) | copy-start | bytes 3145732
  8.1 16.1 %copy-start.11 = (f32[2048]{0:T(1024)S(1)}, f32[2048]{0:T(1024)}, u32[]{:S(2)}) copy-start(f32[2048]{0:T(1024)} %param.19) | copy-start | bytes 24580
  19.2 4.9 copy-start.9
  19.2 5.4 copy-start.10
  24.1 28.8 %copy-start.6 = (s32[256]{0:T(256)S(1)}, s32[256]{0:T(256)}, u32[]{:S(2)}) copy-start(s32[256]{0:T(256)} %param.28) | copy-start | bytes 3076
  55.4 14.0 %copy-start.7 = (s32[256]{0:T(256)S(1)}, s32[256]{0:T(256)}, u32[]{:S(2)}) copy-start(s32[256]{0:T(256)} %param.29) | copy-start | bytes 3076
  98.0 178.5 %all-reduce.6.cloned.1.call-start = ((), (), s32[]{:S(2)}) async-start(), calls=%async_computation.1 | async-start | bytes 4194304 | tf_op jit(solution)/shard_map/psum | solution.py:136
  166.8 4.9 copy-start.3
  171.7 204.0 %copy-start.12 = (f32[2048]{0:T(1024)S(1)}, f32[2048]{0:T(1024)}, u32[]{:S(2)}) copy-start(f32[2048]{0:T(1024)} %param.30) | copy-start | bytes 24580
  171.7 192.4 %all-gather.6.cloned.1.call-start = ((), (), s32[]{:S(2)}) async-start(), calls=%async_computation.2 | async-start | bytes 4325376 | tf_op jit(solution)/shard_map/all_gather | solution.py:140
  278.2 192.5 %all-reduce.8.cloned.1.call-start = ((), (), s32[]{:S(2)}) async-start(), calls=%async_computation.5 | async-start | bytes 7340032 | tf_op jit(solution)/shard_map/psum | solution.py:147
  375.7 6.4 copy-start.4
  375.7 6.4 copy-start.8
  385.6 279.0 %reduce-scatter.2.cloned.1.call-start = ((), (), s32[]{:S(2)}) async-start(), calls=%async_computation.3 | async-start | bytes 8650752 | tf_op jit(solution)/shard_map/reduce_scatter | solution.py:149
  478.9 187.3 %copy-start.1 = (bf16[2,4096,128]{2,1,0:T(8,128)(2,1)S(1)}, bf16[2,4096,128]{2,1,0:T(8,128)(2,1)}, u32[]{:S(2)}) copy-start(bf16[2,4096,128]{2,1,0:T(8,128)(2,1)} %param.24) | copy-start | bytes 6291460
  478.9 185.7 %copy-start.5 = (bf16[32,2048]{1,0:T(8,128)(2,1)S(1)}, bf16[32,2048]{1,0:T(8,128)(2,1)}, u32[]{:S(2)}) copy-start(bf16[32,2048]{1,0:T(8,128)(2,1)} %add_convert_fusion.1) | copy-start | bytes 393220
Sparse Core Ops, SparseCore 0:
  98.1 59.2 all-gather.7
  171.8 104.5 all-reduce.5
  278.3 85.8 all-gather.5
  385.7 84.8 all-reduce.7
  479.1 185.5 reduce-scatter.1
where the time goes:
time: 673 us
  waiting for transfers between devices  477 us (71%)
  blocking collectives  69.7 us (10%)
  matrix products  65.4 us (10%)
  other arithmetic  34.3 us (5%)
  between operations  13.5 us (2%)
  local copies, waits for them, and re-layouts  12.8 us (2%)
    reduce_scatter x1, waiting for transfers between devices, body(): lax.psum_scatter(jnp.dot(act, w_down, preferred_element_type=jnp.float32)...  186 us
    psum x1, waiting for transfers between devices, body(): summed = lax.psum(partial_out, 'tp')  103 us
    all_gather x1, waiting for transfers between devices, body(): gathered = lax.all_gather(middle, ('pool', 'tp'), axis=0, tiled=True)  85.9 us
    psum x1, waiting for transfers between devices, body(): gate, upward = lax.psum((part_gate, part_upward), 'grp')  85 us
    psum x1, blocking collectives, body(): lax.psum((part_query, part_key, part_value), 'grp')  26.5 us
    all_gather x2, blocking collectives, joined(): everything = jax.tree.map(lambda part: lax.all_gather(part, axis), array)  25.2 us
    all_gather x1, waiting for transfers between devices, joined(): everything = jax.tree.map(lambda part: lax.all_gather(part, axis), array)  16.9 us
    reduce_sum x1, other arithmetic, body(): pre_weights.astype(jnp.float32).sum(axis=4)  14.6 us
  transfers between devices with their start and end apart: 5, of which 5 were waited for; matrix products, arithmetic and copies ran while one was open for 3% of the time, Pallas kernels for 0%

commit v1 on v0

--- a/solution.py
+++ b/solution.py
@@ -133,7 +133,8 @@
     partial_out = jnp.dot(attended, w_out, preferred_element_type=jnp.float32)
     share = stream_count // lax.axis_size("tp")
     tp_start = lax.axis_index("tp") * share
-    summed = lax.psum(partial_out, "tp")
+    shards = lax.all_gather(partial_out, "tp", axis=0, tiled=False)
+    summed = shards.sum(axis=0)
     summed = lax.dynamic_slice_in_dim(summed, tp_start, share, 0)
     own_hidden = lax.dynamic_slice_in_dim(hidden_float, tp_start, share, 0)
     middle = (own_hidden + summed).astype(jnp.bfloat16)

time: 673 us -> 903 us (1.34)
  waiting for transfers between devices: 477 us -> 699 us
    all_gather x0 -> x1, waiting for transfers between devices: none -> 324 us  [body(): shards = lax.all_gather(partial_out, 'tp', axis=0, tiled=False)]
    psum x1 -> x0, waiting for transfers between devices: 103 us -> none  [body(): summed = lax.psum(partial_out, 'tp')]
  transfers between devices with their start and end apart: 5 -> 5, of which waited for: 5 -> 5; matrix products, arithmetic and copies ran while one was open for 3% -> 2% of each run, Pallas kernels for 0% -> 0%
where the time goes in v1:
time: 903 us; the launch traced here: 902 us
  waiting for transfers between devices  699 us (77%)
  blocking collectives  69.7 us (8%)
  matrix products  64.4 us (7%)
  other arithmetic  42 us (5%)
  between operations  13.5 us (1%)
  local copies, waits for them, and re-layouts  12.8 us (1%)
    all_gather x1, waiting for transfers between devices, body(): shards = lax.all_gather(partial_out, 'tp', axis=0, tiled=False)  324 us
    reduce_scatter x1, waiting for transfers between devices, body(): lax.psum_scatter(jnp.dot(act, w_down, preferred_element_type=jnp.float32)...  186 us
    all_gather x1, waiting for transfers between devices, body(): gathered = lax.all_gather(middle, ('pool', 'tp'), axis=0, tiled=True)  87.3 us
    psum x1, waiting for transfers between devices, body(): gate, upward = lax.psum((part_gate, part_upward), 'grp')  84.7 us
    psum x1, blocking collectives, body(): lax.psum((part_query, part_key, part_value), 'grp')  26.5 us
    all_gather x2, blocking collectives, joined(): everything = jax.tree.map(lambda part: lax.all_gather(part, axis), array)  25.2 us
  transfers between devices with their start and end apart: 5, of which 5 were waited for; matrix products, arithmetic and copies ran while one was open for 2% of the time, Pallas kernels for 0%

profile of v1, /device:TPU:1, one launch (start us, length us, event | category | flops | bytes accessed | tf_op | source)
XLA Modules:
  0.0 902.2 jit_solution(10086700921107988655)
XLA Ops:
  6.5 0.8 fusion.59
  7.4 0.7 broadcast_subtract_fusion
  8.1 1.6 multiply_reduce_fusion
  9.7 9.5 %psum.49 = f32[256]{0:T(256)S(1)} all-reduce(f32[256]{0:T(256)S(1)} %multiply_reduce_fusion), channel_id=1, replica_groups=mesh['pool'=4,'grp'=4,'tp'=8] {'grp'}, use_global_device_ids=true, to_apply=%region_1.0 | all-reduce | flops 256 | bytes 2048 | tf_op jit(solution)/shard_map/psum | solution.py:53
  19.2 4.9 fusion.46
  24.1 0.5 fusion.45
  24.7 0.5 fusion.44
  25.2 26.5 %all-reduce.6 = (bf16[256,1024]{1,0:T(8,128)(2,1)S(1)}, bf16[256,128]{1,0:T(8,128)(2,1)S(1)}, bf16[256,128]{1,0:T(8,128)(2,1)S(1)}) all-reduce(f32[256,1024]{1,0:T(8,128)} %fusion.46, f32[256,128]{1,0:T(8,128)S(1)} %fusion.45, f32[256,128]{1,0:T(8,128)S(1)} %fusion.44), channel_id=1, replica_groups=mesh['pool'=4,'grp'=4,'tp'=8] {'grp'}, use_global_device_ids=true, to_apply=%region_2.0 | all-reduce | flops 327680 | bytes 1966080 | tf_op jit(solution)/shard_map/psum | solution.py:59
  51.7 0.1 copy.64
  51.8 0.6 reduce-window.6
  52.4 0.2 slice_reduce_fusion
  52.6 0.2 reduce-window.9
  53.0 1.6 scatter_custom_fusion
  54.6 0.8 gather_fusion
  55.4 13.1 %bitcast_reduce_fusion = (f32[2,128,8]{1,2,0:T(8,128)S(1)}, f32[2,128,8,4096]{3,1,2,0:T(8,128)}) fusion(bf16[2,4096,128]{2,1,0:T(8,128)(2,1)S(1)} %copy-done, bf16[2,128,8,128]{3,2,1,0:T(8,128)(2,1)S(1)} %bitcast.167), kind=kOutput, calls=%fused_computation.17 | convolution fusion | flops 2164258816 | bytes 36184064 | tf_op jit(solution)/shard_map/pskgd,pjkd->pskgj/dot_general | solution.py:89
  68.5 0.1 copy.47
  68.6 0.7 gather_fusion.1
  69.4 0.1 broadcast_compare_fusion
  69.5 4.5 fusion.47
  74.1 0.7 gather_fusion.2
  74.9 13.8 %fusion.17 = f32[2,128,1,8,128]{4,1,3,0,2:T(8,128)S(1)} fusion(bf16[2,4096,128]{2,1,0:T(8,128)(2,1)} %param.25, f32[2,128,8]{1,2,0:T(8,128)S(1)} %copy.48, f32[2,128,8,4096]{3,1,2,0:T(8,128)} %get-tuple-element.234), kind=kOutput, calls=%fused_computation.37 | convolution fusion | flops 2172649472 | bytes 36708352 | tf_op jit(solution)/shard_map/pskgj,pjkd->pskgd/dot_general | solution.py:105
  88.7 1.6 copy.50
  90.3 2.9 gather_fusion.4
  93.2 4.7 convolution_add_fusion
  98.0 10.4 %all-gather.2 = f32[1024,8]{1,0:T(8,128)S(1)} all-gather(f32[256,8]{1,0:T(8,128)S(1)} %max.43), channel_id=4, replica_groups=mesh['pool'=4,'grp'=4,'tp'=8] {'grp'}, dimensions={0}, use_global_device_ids=true | all-gather | bytes 40960 | tf_op jit(solution)/shard_map/all_gather | solution.py:13
  108.5 14.6 %convert_reduce_fusion = f32[2,128,8]{1,2,0:T(8,128)S(1)} fusion(f32[2,128,8]{1,2,0:T(8,128)S(1)} %copy.48, f32[2,128,8,4096]{3,1,2,0:T(8,128)} %get-tuple-element.234), kind=kLoop, calls=%fused_computation.20 | loop fusion | flops 41940992 | bytes 33570816 | tf_op jit(solution)/shard_map/reduce_sum | solution.py:103
  123.2 0.1 copy.49
  123.3 0.7 gather_fusion.3
  124.0 0.7 convert_reduce_fusion.1
  124.8 14.8 %all-gather.3 = f32[1024,8]{1,0:T(8,128)S(1)} all-gather(f32[256,8]{1,0:T(8,128)S(1)} %add.160), channel_id=5, replica_groups=mesh['pool'=4,'grp'=4,'tp'=8] {'grp'}, dimensions={0}, use_global_device_ids=true | all-gather | bytes 40960 | tf_op jit(solution)/shard_map/all_gather | solution.py:13
  139.7 0.2 copy.54
  139.8 0.2 copy.55
  140.0 0.4 fusion.32
  140.5 16.9 %all-gather.10.cloned.1.call-done = f32[1024,8,128]{2,1,0:T(8,128)} async-done(((f32[256,8,128]{2,1,0:T(8,128)}), f32[1024,8,128]{2,1,0:T(8,128)}) %all-gather.10.cloned.1.call-update) | async-done | bytes 4194320 | tf_op jit(solution)/shard_map/all_gather | solution.py:13
  157.4 1.3 slice_bitcast_fusion
  158.7 6.7 while.19
  158.8 0.1 copy.80
  158.9 0.1 copy.81
  159.0 1.9 fusion.65
  161.0 0.1 copy.80
  161.1 0.1 copy.81
  161.3 1.9 fusion.65
  163.3 0.1 copy.80
  163.4 0.1 copy.81
  163.5 1.9 fusion.65
  165.4 0.1 copy.59
  165.6 0.1 copy.58
  165.7 0.1 copy.57
  165.8 1.0 divide_convert_fusion
  166.9 4.9 fusion.28
  171.8 1.5 convert_element_type.68
  173.4 324.4 %all-gather.12.cloned.1.call-done = f32[2048,2048]{1,0:T(8,128)} async-done(((f32[256,2048]{1,0:T(8,128)}), f32[2048,2048]{1,0:T(8,128)}) %all-gather.12.cloned.1.call-update) | async-done | bytes 16777232 | tf_op jit(solution)/shard_map/all_gather | solution.py:136
  497.8 7.8 reduce_sum.61
  505.6 1.6 add_convert_fusion.1
  507.3 87.3 %all-gather.8.cloned.1.call-done = bf16[1024,2048]{1,0:T(8,128)(2,1)} async-done(((bf16[32,2048]{1,0:T(8,128)(2,1)}), bf16[1024,2048]{1,0:T(8,128)(2,1)}) %all-gather.8.cloned.1.call-update) | async-done | bytes 4194320 | tf_op jit(solution)/shard_map/all_gather | solution.py:141
  594.6 3.1 fusion.9
  597.7 8.5 psum.53
  606.2 5.8 fusion.22
  612.0 3.5 fusion.24
  615.5 0.3 reduce-scatter.2.cloned.1.call-start
  615.8 84.7 %all-reduce.5.cloned.1.call-done = (f32[1024,448]{0,1:T(8,128)}, f32[1024,448]{0,1:T(8,128)}) async-done(((f32[1024,448]{0,1:T(8,128)}, f32[1024,448]{0,1:T(8,128)}), (f32[1024,448]{0,1:T(8,128)}, f32[1024,448]{0,1:T(8,128)})) %all-reduce.5.cloned.1.call-update) | async-done | bytes 3670032 | tf_op jit(solution)/shard_map/psum | solution.py:148
  700.6 7.7 fusion.26
  708.3 185.7 %reduce-scatter.2.cloned.1.call-done = f32[32,2048]{1,0:T(8,128)} async-done(((f32[1024,2048]{1,0:T(8,128)}), f32[32,2048]{1,0:T(8,128)}) %reduce-scatter.2.cloned.1.call-update) | async-done | bytes 262160 | tf_op jit(solution)/shard_map/reduce_scatter | solution.py:150
  894.0 1.6 add_convert_fusion
  (69 shorter events, 0.9 us)
Async XLA Ops:
  6.5 48.9 %copy-start = (bf16[2,4096,128]{2,1,0:T(8,128)(2,1)S(1)}, bf16[2,4096,128]{2,1,0:T(8,128)(2,1)}, u32[]{:S(2)}) copy-start(bf16[2,4096,128]{2,1,0:T(8,128)(2,1)} %param.24) | copy-start | bytes 6291460
  6.5 150.9 %all-gather.10.cloned.1.call-start = ((), (), s32[]{:S(2)}) async-start(), calls=%async_computation.3 | async-start | bytes 5242880 | tf_op jit(solution)/shard_map/all_gather | solution.py:13
  8.1 16.1 %copy-start.2 = (bf16[256,2048]{1,0:T(8,128)(2,1)S(1)}, bf16[256,2048]{1,0:T(8,128)(2,1)}, u32[]{:S(2)}) copy-start(bf16[256,2048]{1,0:T(8,128)(2,1)} %param.18) | copy-start | bytes 3145732
  8.1 16.1 %copy-start.13 = (f32[2048]{0:T(1024)S(1)}, f32[2048]{0:T(1024)}, u32[]{:S(2)}) copy-start(f32[2048]{0:T(1024)} %param.19) | copy-start | bytes 24580
  19.2 4.9 copy-start.11
  19.2 5.4 copy-start.12
  24.1 28.8 %copy-start.6 = (s32[256]{0:T(256)S(1)}, s32[256]{0:T(256)}, u32[]{:S(2)}) copy-start(s32[256]{0:T(256)} %param.28) | copy-start | bytes 3076
  55.4 14.0 %copy-start.7 = (s32[256]{0:T(256)S(1)}, s32[256]{0:T(256)}, u32[]{:S(2)}) copy-start(s32[256]{0:T(256)} %param.29) | copy-start | bytes 3076
  98.0 399.8 %all-gather.12.cloned.1.call-start = ((), (), s32[]{:S(2)}) async-start(), calls=%async_computation.4 | async-start | bytes 18874368 | tf_op jit(solution)/shard_map/all_gather | solution.py:136
  166.8 5.0 copy-start.3
  171.8 422.9 %all-gather.8.cloned.1.call-start = ((), (), s32[]{:S(2)}) async-start(), calls=%async_computation.1 | async-start | bytes 4325376 | tf_op jit(solution)/shard_map/all_gather | solution.py:141
  505.6 100.6 %copy-start.14 = (f32[2048]{0:T(1024)S(1)}, f32[2048]{0:T(1024)}, u32[]{:S(2)}) copy-start(f32[2048]{0:T(1024)} %param.30) | copy-start | bytes 24580
  507.2 98.9 %copy-start.8 = (bf16[2048,448]{0,1:T(8,128)(2,1)S(1)}, bf16[2048,448]{0,1:T(8,128)(2,1)}, u32[]{:S(2)}) copy-start(bf16[2048,448]{0,1:T(8,128)(2,1)} %param.32) | copy-start | bytes 5505028
  507.3 193.3 %all-reduce.5.cloned.1.call-start = ((), (), s32[]{:S(2)}) async-start(), calls=%async_computation.5 | async-start | bytes 7340032 | tf_op jit(solution)/shard_map/psum | solution.py:148
  606.2 5.8 copy-start.4
  606.2 5.8 copy-start.9
  612.0 88.6 %copy-start.10 = (bf16[448,2048]{1,0:T(8,128)(2,1)S(1)}, bf16[448,2048]{1,0:T(8,128)(2,1)}, u32[]{:S(2)}) copy-start(bf16[448,2048]{1,0:T(8,128)(2,1)} %param.33) | copy-start | bytes 5505028
  615.5 278.5 %reduce-scatter.2.cloned.1.call-start = ((), (), s32[]{:S(2)}) async-start(), calls=%async_computation.2 | async-start | bytes 8650752 | tf_op jit(solution)/shard_map/reduce_scatter | solution.py:150
  708.3 187.3 %copy-start.1 = (bf16[2,4096,128]{2,1,0:T(8,128)(2,1)S(1)}, bf16[2,4096,128]{2,1,0:T(8,128)(2,1)}, u32[]{:S(2)}) copy-start(bf16[2,4096,128]{2,1,0:T(8,128)(2,1)} %param.24) | copy-start | bytes 6291460
  708.3 185.7 %copy-start.5 = (bf16[32,2048]{1,0:T(8,128)(2,1)S(1)}, bf16[32,2048]{1,0:T(8,128)(2,1)}, u32[]{:S(2)}) copy-start(bf16[32,2048]{1,0:T(8,128)(2,1)} %add_convert_fusion.1) | copy-start | bytes 393220
Sparse Core Ops, SparseCore 0:
  98.1 59.2 all-gather.9
  171.9 325.8 all-gather.11
  507.4 87.2 all-gather.7
  615.6 84.8 all-reduce.4
  708.5 185.5 reduce-scatter.1
